TPU v7x, 256 devices: a whole 4x4x8 slice. The times are simulated.
256 devices in a mesh: dp: 32 (over z, x), et: 8 (over y, core).
Axes of the slice: x: 4, y: 4, z: 8, core: 2. Of those that a mesh axis runs over, the one named last changes fastest.
Arguments:
- tokens: bfloat16 [4096, 2048], P('dp', 'et'), may hold values from -6 to 6
- cotangent: bfloat16 [4096, 2048], P('dp', 'et'), may hold values from -1.5 to 1.5
- expert_ids: int32 [4096, 8], P('dp'), may hold values from 0 to 63, all different within a row; in each aligned block of 128 rows (0 to 127, 128 to 255, ...) at most 24 rows name the same one
- route_gates: bfloat16 [4096, 8], P('dp'), may hold values from 0.049804688 to 0.3984375
- gate_proj: bfloat16 [64, 2048, 1024], P('dp', None, 'et'), may hold values from -0.125 to 0.125
- up_proj: bfloat16 [64, 2048, 1024], P('dp', None, 'et'), may hold values from -0.125 to 0.125
- down_proj: bfloat16 [64, 1024, 2048], P('dp', 'et'), may hold values from -0.1875 to 0.1875
Outputs:
- mixed: bfloat16 [4096, 2048], P('dp', 'et')
- grad_tokens: bfloat16 [4096, 2048], P('dp', 'et')
- grad_gates: float32 [4096, 8], P('dp')
- grad_gate_proj: float32 [64, 2048, 1024], P('dp', None, 'et')
- grad_up_proj: float32 [64, 2048, 1024], P('dp', None, 'et')
- grad_down_proj: float32 [64, 1024, 2048], P('dp', 'et')
Inputs may be any that keep to these rules, and one draw needn't show every extreme that they name: `expert_ids`: each row names 8 different experts. Among the rows of one device (128 aligned rows), no expert is named more than 24 times, a bound that some block reaches.
All inputs are finite; a program needn't handle non-finite values.
Results may differ from a plain program's by a relative error of at most 0.015.
Values may be sent and summed in bfloat16 or wider, within the bound.
No kernel may reach another device: no remote copies, remote signals or barrier semaphores. Data moves between devices by JAX's collectives and lax.ppermute only.
A program may use at most 128 MiB of HBM per device.

v0:
```python
import jax
import jax.numpy as jnp
from jax import lax
from jax.sharding import PartitionSpec as P


def places_in_block(chosen, experts):
    flattened = chosen.reshape(-1)
    pairs = flattened.shape[0]
    onehot = (flattened[:, None] == jnp.arange(experts, dtype=jnp.int32)[None, :]).astype(
        jnp.bfloat16
    )
    rows = lax.broadcasted_iota(jnp.int32, (pairs, pairs), 0)
    cols = lax.broadcasted_iota(jnp.int32, (pairs, pairs), 1)
    earlier = (cols < rows).astype(jnp.bfloat16)
    before = jnp.dot(earlier, onehot, preferred_element_type=jnp.float32)
    return jnp.sum(before * onehot.astype(jnp.float32), axis=1).astype(jnp.int32)


def local(tokens, cotangent, expert_ids, route_gates, gate_proj, up_proj, down_proj):
    groups = lax.axis_size("dp")
    shards = lax.axis_size("et")
    local_experts, features, units = gate_proj.shape
    experts = local_experts * groups
    tok_rows, per_token = expert_ids.shape
    width = tokens.shape[1]
    capacity = 3 * tok_rows * per_token // (2 * experts)
    slots = experts * capacity
    places = places_in_block(expert_ids, experts)
    slot_index = (expert_ids.reshape(-1) * capacity + places).reshape(tok_rows, per_token)
    pairs = tok_rows * per_token
    pair_slot = (
        slot_index.reshape(pairs, 1) == jnp.arange(slots, dtype=jnp.int32)[None, :]
    ).astype(jnp.bfloat16)
    owner = lax.broadcasted_iota(
        jnp.int32, (tok_rows, pairs), 1
    ) // per_token == lax.broadcasted_iota(jnp.int32, (tok_rows, pairs), 0)
    gate_owner = jnp.where(owner, route_gates.reshape(1, pairs), jnp.zeros((), jnp.bfloat16))
    select = jnp.einsum(
        "tp,ps->st", owner.astype(jnp.bfloat16), pair_slot, preferred_element_type=jnp.float32
    ).astype(jnp.bfloat16)
    gate_select = jnp.einsum(
        "tp,ps->st", gate_owner, pair_slot, preferred_element_type=jnp.float32
    ).astype(jnp.bfloat16)
    picked = jnp.dot(select, tokens, preferred_element_type=jnp.float32).astype(jnp.bfloat16)
    scaled = jnp.dot(gate_select, cotangent, preferred_element_type=jnp.float32).astype(
        jnp.bfloat16
    )
    expert_in_part, expert_cot_part = (
        lax.all_to_all(
            picked.reshape(experts, capacity, width), "dp", split_axis=0, concat_axis=1, tiled=True
        ),
        lax.all_to_all(
            scaled.reshape(experts, capacity, width), "dp", split_axis=0, concat_axis=1, tiled=True
        ),
    )
    expert_in = lax.all_gather(expert_in_part, "et", axis=0)
    expert_cot = lax.all_gather(expert_cot_part, "et", axis=0)
    gate_w = gate_proj.reshape(local_experts, shards, width, units)
    up_w = up_proj.reshape(local_experts, shards, width, units)
    down_w = down_proj.reshape(local_experts, units, shards, width)
    pre_gate = jnp.einsum("jesd,ejdf->esf", expert_in, gate_w, preferred_element_type=jnp.float32)
    pre_up = jnp.einsum("jesd,ejdf->esf", expert_in, up_w, preferred_element_type=jnp.float32)
    sigmoid_gate = jax.nn.sigmoid(pre_gate)
    silu_gate = pre_gate * sigmoid_gate
    hidden = (silu_gate * pre_up).astype(jnp.bfloat16)
    out_part = jnp.einsum("esf,efd->esd", hidden, down_proj, preferred_element_type=jnp.float32)
    grad_hidden = jnp.einsum(
        "jesd,efjd->esf", expert_cot, down_w, preferred_element_type=jnp.float32
    )
    grad_pre_gate = (
        grad_hidden * pre_up * sigmoid_gate * (1.0 + pre_gate * (1.0 - sigmoid_gate))
    ).astype(jnp.bfloat16)
    grad_pre_up = (grad_hidden * silu_gate).astype(jnp.bfloat16)
    grad_down = jnp.einsum(
        "esf,jesd->efjd", hidden, expert_cot, preferred_element_type=jnp.float32
    ).reshape(local_experts, units, features)
    grad_gate_w = jnp.einsum(
        "jesd,esf->ejdf", expert_in, grad_pre_gate, preferred_element_type=jnp.float32
    ).reshape(local_experts, features, units)
    grad_up_w = jnp.einsum(
        "jesd,esf->ejdf", expert_in, grad_pre_up, preferred_element_type=jnp.float32
    ).reshape(local_experts, features, units)
    in_part = jnp.einsum(
        "esf,edf->esd", grad_pre_gate, gate_proj, preferred_element_type=jnp.float32
    )
    in_part = in_part + jnp.einsum(
        "esf,edf->esd", grad_pre_up, up_proj, preferred_element_type=jnp.float32
    )
    out_sum = lax.psum_scatter(out_part.astype(jnp.bfloat16), "et", scatter_dimension=2, tiled=True)
    in_part, grad_gate_w, grad_up_w, grad_down = lax.optimization_barrier(
        (in_part.astype(jnp.bfloat16), grad_gate_w, grad_up_w, grad_down)
    )
    in_sum = lax.psum_scatter(in_part, "et", scatter_dimension=2, tiled=True)
    back_out, back_grad = (
        lax.all_to_all(out_sum, "dp", split_axis=1, concat_axis=0, tiled=True),
        lax.all_to_all(in_sum, "dp", split_axis=1, concat_axis=0, tiled=True),
    )
    back_out = back_out.reshape(slots, width)
    back_grad = back_grad.reshape(slots, width)
    mixed = jnp.einsum(
        "st,sd->td", gate_select, back_out, preferred_element_type=jnp.float32
    ).astype(jnp.bfloat16)
    grad_tokens = jnp.einsum(
        "st,sd->td", select, back_grad, preferred_element_type=jnp.float32
    ).astype(jnp.bfloat16)
    out_rows = (
        back_out[slot_index.reshape(-1)].reshape(tok_rows, per_token, width).astype(jnp.float32)
    )
    gate_part = jnp.sum(cotangent.astype(jnp.float32)[:, None, :] * out_rows, axis=2)
    grad_gates = lax.psum(gate_part, "et")
    return (mixed, grad_tokens, grad_gates, grad_gate_w, grad_up_w, grad_down)


def solution(mesh):
    in_specs = (
        P("dp", "et"),
        P("dp", "et"),
        P("dp", None),
        P("dp", None),
        P("dp", None, "et"),
        P("dp", None, "et"),
        P("dp", "et", None),
    )
    out_specs = (
        P("dp", "et"),
        P("dp", "et"),
        P("dp", None),
        P("dp", None, "et"),
        P("dp", None, "et"),
        P("dp", "et", None),
    )
    return jax.shard_map(local, mesh=mesh, in_specs=in_specs, out_specs=out_specs, check_vma=False)
```

profile of v0, /device:TPU:2, one launch (start us, length us, event | category | flops | bytes accessed | tf_op | source)
XLA Modules:
  0.0 295.2 jit_solution(13721810918180096629)
XLA Ops:
  10.5 33.9 %all_to_all.60 = bf16[64,24,256]{2,1,0:T(8,128)(2,1)S(1)} all-to-all(bf16[64,24,256]{2,1,0:T(8,128)(2,1)S(1)} %bitcast.93), channel_id=1, replica_groups=mesh['dp'=32,'et'=8] {'dp'}, dimensions={0} | all-to-all | bytes 1572864 | tf_op jit(solution)/shard_map/all_to_all | solution.py:50
  47.2 26.7 %all_to_all.61 = bf16[64,24,256]{2,1,0:T(8,128)(2,1)S(1)} all-to-all(bf16[64,24,256]{2,1,0:T(8,128)(2,1)S(1)} %bitcast.94), channel_id=1, replica_groups=mesh['dp'=32,'et'=8] {'dp'}, dimensions={0} | all-to-all | bytes 1572864 | tf_op jit(solution)/shard_map/all_to_all | solution.py:53
  74.9 10.9 %all-gather.3.cloned.1.call-done = bf16[8,2,768,256]{3,2,0,1:T(8,128)(2,1)} async-done(((bf16[1,2,768,256]{3,2,0,1:T(8,128)(2,1)}), bf16[8,2,768,256]{3,2,0,1:T(8,128)(2,1)}) %all-gather.3.cloned.1.call-update) | async-done | bytes 6291472 | tf_op jit(solution)/shard_map/all_gather | solution.py:57
  85.8 5.6 %convolution_bitcast_fusion.1 = f32[2,768,128]{2,1,0:T(8,128)} fusion(bf16[8,2,768,256]{3,2,0,1:T(8,128)(2,1)} %all-gather.3.cloned.1.call-done, bf16[2,8,256,128]{3,2,1,0:T(8,128)(2,1)S(1)} %bitcast.86), kind=kOutput, calls=%fused_computation.16 | convolution fusion | flops 805306368 | bytes 8126464 | tf_op jit(solution)/shard_map/jesd,ejdf->esf/dot_general | solution.py:63
  91.4 2.7 convolution_bitcast_fusion.2
  94.1 37.7 %all-gather.5.cloned.1.call-done = bf16[8,2,768,256]{3,2,0,1:T(8,128)(2,1)} async-done(((bf16[1,2,768,256]{3,2,0,1:T(8,128)(2,1)}), bf16[8,2,768,256]{3,2,0,1:T(8,128)(2,1)}) %all-gather.5.cloned.1.call-update) | async-done | bytes 6291472 | tf_op jit(solution)/shard_map/all_gather | solution.py:58
  131.7 5.7 %multiply_convert_fusion = (bf16[2,768,128]{2,1,0:T(8,128)(2,1)}, bf16[2,768,128]{2,1,0:T(8,128)(2,1)S(1)}, bf16[2,768,128]{2,1,0:T(8,128)(2,1)S(1)}) fusion(f32[2,768,128]{2,1,0:T(8,128)} %convolution_bitcast_fusion.2, f32[2,768,128]{2,1,0:T(8,128)S(1)} %copy-done.11, bf16[8,2,768,256]{3,2,0,1:T(8,128)(2,1)} %all-gather.5.cloned.1.call-done, ...), kind=kOutput, calls=%fused_computation.26 | convolution fusion | flops 808255488 | bytes 10092544 | tf_op jit(solution)/shard_map/jesd,efjd->esf/dot_general | solution.py:68
  138.2 4.4 %convolution_convert_fusion = bf16[2,768,2048]{2,1,0:T(8,128)(2,1)} fusion(bf16[2,768,128]{2,1,0:T(8,128)(2,1)S(1)} %get-tuple-element.34, bf16[2,128,2048]{2,1,0:T(8,128)(2,1)S(1)} %copy-done.10), kind=kOutput, calls=%fused_computation.4 | convolution fusion | flops 808452096 | bytes 7733248 | tf_op jit(solution)/shard_map/esf,efd->esd/dot_general | solution.py:67
  142.9 5.6 %fusion.21 = f32[2,128,8,256]{1,3,2,0:T(8,128)S(1)} fusion(bf16[8,2,768,256]{3,2,0,1:T(8,128)(2,1)} %all-gather.5.cloned.1.call-done, bf16[2,768,128]{2,1,0:T(8,128)(2,1)} %copy-done.9), kind=kOutput, calls=%fused_computation.33 | convolution fusion | flops 805306368 | bytes 8781824 | tf_op jit(solution)/shard_map/esf,jesd->efjd/dot_general | solution.py:75
  148.5 6.8 %fusion.23 = f32[2,8,256,128]{3,2,1,0:T(8,128)} fusion(bf16[8,2,768,256]{3,2,0,1:T(8,128)(2,1)} %all-gather.3.cloned.1.call-done, bf16[2,768,128]{2,1,0:T(8,128)(2,1)} %get-tuple-element.32), kind=kOutput, calls=%fused_computation.35 | convolution fusion | flops 805306368 | bytes 8781824 | tf_op jit(solution)/shard_map/jesd,esf->ejdf/dot_general | solution.py:81
  155.3 4.0 %fusion.25 = f32[2,8,256,128]{3,2,1,0:T(8,128)} fusion(bf16[8,2,768,256]{3,2,0,1:T(8,128)(2,1)S(1)} %bitcast.82, bf16[2,768,128]{2,1,0:T(8,128)(2,1)S(1)} %get-tuple-element.33), kind=kOutput, calls=%fused_computation.37 | convolution fusion | flops 805306368 | bytes 8781824 | tf_op jit(solution)/shard_map/jesd,esf->ejdf/dot_general | solution.py:78
  159.3 1.8 fusion.42
  161.1 4.5 %add_convert_fusion = bf16[2,768,2048]{2,1,0:T(8,128)(2,1)} fusion(f32[2,768,2048]{2,1,0:T(8,128)S(1)} %fusion.42, bf16[2,768,128]{2,1,0:T(8,128)(2,1)S(1)} %copy-done.8, bf16[2,2048,128]{2,1,0:T(8,128)(2,1)S(1)} %copy-done.3), kind=kOutput, calls=%fused_computation.1 | convolution fusion | flops 811597824 | bytes 20316160 | tf_op jit(solution)/shard_map/esf,edf->esd/dot_general | solution.py:87
  165.6 22.3 %reduce-scatter.3.cloned.1.call-done = bf16[2,768,256]{2,1,0:T(8,128)(2,1)} async-done(((bf16[2,768,2048]{2,1,0:T(8,128)(2,1)}), bf16[2,768,256]{2,1,0:T(8,128)(2,1)}) %reduce-scatter.3.cloned.1.call-update) | async-done | bytes 786448 | tf_op jit(solution)/shard_map/reduce_scatter | solution.py:90
  187.9 3.0 %copy.51 = bf16[2,768,256]{2,0,1:T(2,128)(2,1)} copy(bf16[2,768,256]{2,1,0:T(8,128)(2,1)} %reduce-scatter.3.cloned.1.call-done) | data formatting | bytes 1572864 | tf_op jit(solution)/shard_map/reduce_scatter | solution.py:90
  190.9 10.2 %all-to-all-start.1 = ((bf16[2,768,256]{2,0,1:T(2,128)(2,1)}), bf16[2,768,256]{2,0,1:T(2,128)(2,1)}, u32[]{:S(2)}, u32[]{:S(2)}) async-start(bf16[2,768,256]{2,0,1:T(2,128)(2,1)} %copy.51), calls=%async_computation.2 | async-start | bytes 1572864 | tf_op jit(solution)/shard_map/all_to_all | solution.py:96
  201.1 34.5 %reduce-scatter.5.cloned.1.call-done = bf16[2,768,256]{2,1,0:T(8,128)(2,1)} async-done(((bf16[2,768,2048]{2,1,0:T(8,128)(2,1)}), bf16[2,768,256]{2,1,0:T(8,128)(2,1)}) %reduce-scatter.5.cloned.1.call-update) | async-done | bytes 786448 | tf_op jit(solution)/shard_map/reduce_scatter | solution.py:94
  235.7 2.8 copy.59
  238.5 10.3 %all-to-all-start.3 = ((bf16[2,768,256]{2,0,1:T(2,128)(2,1)}), bf16[2,768,256]{2,0,1:T(2,128)(2,1)}, u32[]{:S(2)}, u32[]{:S(2)}) async-start(bf16[2,768,256]{2,0,1:T(2,128)(2,1)} %copy.59), calls=%async_computation.5 | async-start | bytes 1572864 | tf_op jit(solution)/shard_map/all_to_all | solution.py:97
  248.8 1.5 convert_element_type.85
  252.0 1.8 copy.64
  253.8 1.3 copy.52
  255.1 3.9 %gather_fusion = bf16[1024,256]{1,0:T(8,128)(2,1)S(1)} fusion(bf16[1536,256]{1,0:T(8,128)(2,1)S(1)} %bitcast.83, s32[1024]{0:T(1024)S(1)} %broadcast_clamp_fusion), kind=kCustom, calls=%fused_computation | custom fusion | bytes 1052672 | tf_op jit(solution)/shard_map/gather | solution.py:108
  259.3 25.5 %psum.7 = f32[128,8]{1,0:T(8,128)S(1)} all-reduce(f32[128,8]{1,0:T(8,128)S(1)} %fusion.18), channel_id=1, replica_groups=mesh['dp'=32,'et'=8] {'et'}, use_global_device_ids=true, to_apply=%region_4.5 | all-reduce | flops 1024 | bytes 8192 | tf_op jit(solution)/shard_map/psum | solution.py:111
  (75 shorter events, 13.9 us)
Async XLA Ops:
  7.2 84.2 %copy-start = (bf16[2,2048,128]{2,1,0:T(8,128)(2,1)S(1)}, bf16[2,2048,128]{2,1,0:T(8,128)(2,1)}, u32[]{:S(2)}) copy-start(bf16[2,2048,128]{2,1,0:T(8,128)(2,1)} %param.11) | copy-start | bytes 3145732
  7.2 2.9 copy-start.14
  7.2 78.6 %all-gather.3.cloned.1.call-start = ((), (), s32[]{:S(2)}) async-start(), calls=%async_computation.6 | async-start | bytes 7077888 | tf_op jit(solution)/shard_map/all_gather | solution.py:57
  8.2 37.2 %copy-start.16 = (bf16[128,8]{0,1:T(8,128)(2,1)S(1)}, bf16[128,8]{0,1:T(8,128)(2,1)}, u32[]{:S(2)}) copy-start(bf16[128,8]{0,1:T(8,128)(2,1)} %param.10) | copy-start | bytes 6148
  10.1 35.2 %copy-start.4 = (bf16[1536,128]{1,0:T(8,128)(2,1)}, bf16[1536,128]{1,0:T(8,128)(2,1)S(1)}, u32[]{:S(2)}) copy-start(bf16[1536,128]{1,0:T(8,128)(2,1)S(1)} %fusion.11) | copy-start | bytes 1179652
  10.1 36.7 %copy-start.13 = (bf16[128,256]{1,0:T(8,128)(2,1)S(1)}, bf16[128,256]{1,0:T(8,128)(2,1)}, u32[]{:S(2)}) copy-start(bf16[128,256]{1,0:T(8,128)(2,1)} %param.8) | copy-start | bytes 196612
  45.3 40.5 %copy-start.2 = (bf16[2,2048,128]{2,1,0:T(8,128)(2,1)S(1)}, bf16[2,2048,128]{2,1,0:T(8,128)(2,1)}, u32[]{:S(2)}) copy-start(bf16[2,2048,128]{2,1,0:T(8,128)(2,1)} %param.12) | copy-start | bytes 3145732
  45.3 86.4 %all-gather.5.cloned.1.call-start = ((), (), s32[]{:S(2)}) async-start(), calls=%async_computation.8 | async-start | bytes 7077888 | tf_op jit(solution)/shard_map/all_gather | solution.py:58
  46.9 28.0 %copy-start.6 = (bf16[1536,128]{1,0:T(8,128)(2,1)}, bf16[1536,128]{1,0:T(8,128)(2,1)S(1)}, u32[]{:S(2)}) copy-start(bf16[1536,128]{1,0:T(8,128)(2,1)S(1)} %fusion.8) | copy-start | bytes 1179652
  74.9 113.1 %reduce-scatter.3.cloned.1.call-start = ((), (), s32[]{:S(2)}) async-start(), calls=%async_computation.7 | async-start | bytes 7077888 | tf_op jit(solution)/shard_map/reduce_scatter | solution.py:90
  85.8 5.6 %copy-start.1 = (bf16[8,2,768,256]{3,2,0,1:T(8,128)(2,1)S(1)}, bf16[8,2,768,256]{3,2,0,1:T(8,128)(2,1)}, u32[]{:S(2)}) copy-start(bf16[8,2,768,256]{3,2,0,1:T(8,128)(2,1)} %all-gather.3.cloned.1.call-done) | copy-start | bytes 18874372
  85.8 45.9 %copy-start.10 = (bf16[2,128,2048]{2,1,0:T(8,128)(2,1)S(1)}, bf16[2,128,2048]{2,1,0:T(8,128)(2,1)}, u32[]{:S(2)}) copy-start(bf16[2,128,2048]{2,1,0:T(8,128)(2,1)} %param.13) | copy-start | bytes 3145732
  91.4 40.3 %copy-start.11 = (f32[2,768,128]{2,1,0:T(8,128)S(1)}, f32[2,768,128]{2,1,0:T(8,128)}, u32[]{:S(2)}) copy-start(f32[2,768,128]{2,1,0:T(8,128)} %convolution_bitcast_fusion.1) | copy-start | bytes 2359300
  142.6 93.0 %reduce-scatter.5.cloned.1.call-start = ((), (), s32[]{:S(2)}) async-start(), calls=%async_computation.9 | async-start | bytes 7077888 | tf_op jit(solution)/shard_map/reduce_scatter | solution.py:94
  142.8 12.5 %slice-start = ((s8[6291456]{0:T(1024)(128)(4,1)}), s8[4194304]{0:T(1024)(128)(4,1)S(1)}, s32[]{:S(2)}) async-start(s8[6291456]{0:T(1024)(128)(4,1)} %bitcast.81), calls=%async_computation.10 | async-start | bytes 8388608
  148.5 6.8 %slice-start.1 = ((s8[6291456]{0:T(1024)(128)(4,1)}), s8[2097152]{0:T(1024)(128)(4,1)S(1)}, s32[]{:S(2)}) async-start(s8[6291456]{0:T(1024)(128)(4,1)} %bitcast.81), calls=%async_computation.11 | async-start | bytes 4194304
  159.3 1.8 copy-start.3
  159.3 1.8 copy-start.8
  165.6 84.7 %copy-start.15 = (s32[128,8]{0,1:T(8,128)S(1)}, s32[128,8]{0,1:T(8,128)}, u32[]{:S(2)}) copy-start(s32[128,8]{0,1:T(8,128)} %param.9) | copy-start | bytes 12292
  190.9 47.5 %all-to-all-start.1 = ((bf16[2,768,256]{2,0,1:T(2,128)(2,1)}), bf16[2,768,256]{2,0,1:T(2,128)(2,1)}, u32[]{:S(2)}, u32[]{:S(2)}) async-start(bf16[2,768,256]{2,0,1:T(2,128)(2,1)} %copy.51), calls=%async_computation.2 | async-start | bytes 1572864 | tf_op jit(solution)/shard_map/all_to_all | solution.py:96
  238.5 47.0 %copy-start.7 = (bf16[1536,128]{1,0:T(8,128)(2,1)S(1)}, bf16[1536,128]{1,0:T(8,128)(2,1)}, u32[]{:S(2)}) copy-start(bf16[1536,128]{1,0:T(8,128)(2,1)} %copy-done.6) | copy-start | bytes 1179652
  238.5 47.9 %all-to-all-start.3 = ((bf16[2,768,256]{2,0,1:T(2,128)(2,1)}), bf16[2,768,256]{2,0,1:T(2,128)(2,1)}, u32[]{:S(2)}, u32[]{:S(2)}) async-start(bf16[2,768,256]{2,0,1:T(2,128)(2,1)} %copy.59), calls=%async_computation.5 | async-start | bytes 1572864 | tf_op jit(solution)/shard_map/all_to_all | solution.py:97
  253.8 5.3 %copy-start.12 = (f32[128,256]{1,0:T(8,128)S(1)}, f32[128,256]{1,0:T(8,128)}, u32[]{:S(2)}) copy-start(f32[128,256]{1,0:T(8,128)} %convert_element_type.85) | copy-start | bytes 393220
  253.8 33.9 %copy-start.5 = (bf16[1536,128]{1,0:T(8,128)(2,1)S(1)}, bf16[1536,128]{1,0:T(8,128)(2,1)}, u32[]{:S(2)}) copy-start(bf16[1536,128]{1,0:T(8,128)(2,1)} %copy-done.4) | copy-start | bytes 1179652
  (1 other events, 0.7 us)
Sparse Core Ops, SparseCore 0:
  45.4 40.3 all-gather.2
  88.2 43.4 all-gather.4
  142.7 45.1 reduce-scatter.2
  190.3 45.2 reduce-scatter.4
where the time goes:
time: 296 us; the launch traced here: 295 us
  waiting for transfers between devices  105 us (35%)
  blocking collectives  86 us (29%)
  matrix products  46.7 us (16%)
  starting transfers between devices  20.8 us (7%)
  local copies, waits for them, and re-layouts  20.4 us (7%)
  between operations  14.1 us (5%)
    all_gather x1, waiting for transfers between devices, local(): expert_cot = lax.all_gather(expert_cot_part, 'et', axis=0)  37.7 us
    reduce_scatter x1, waiting for transfers between devices, local(): in_sum = lax.psum_scatter(in_part, 'et', scatter_dimension=2, tiled=True)  34.5 us
    all_to_all x1, blocking collectives, local(): lax.all_to_all(picked.reshape(experts, capacity, width), 'dp', split_axis...  33.9 us
    all_to_all x1, blocking collectives, local(): lax.all_to_all(scaled.reshape(experts, capacity, width), 'dp', split_axis...  26.7 us
    psum x1, blocking collectives, local(): grad_gates = lax.psum(gate_part, 'et')  25.5 us
    reduce_scatter x1, waiting for transfers between devices, local(): lax.psum_scatter(out_part.astype(jnp.bfloat16), 'et', scatter_dimension=2...  22.3 us
    all_gather x1, waiting for transfers between devices, local(): expert_in = lax.all_gather(expert_in_part, 'et', axis=0)  10.9 us
    all_to_all x1, starting transfers between devices, local(): lax.all_to_all(in_sum, 'dp', split_axis=1, concat_axis=0, tiled=True)  10.3 us
  transfers between devices with their start and end apart: 6, of which 4 were waited for; matrix products, arithmetic and copies ran while one was open for 17% of the time, Pallas kernels for 0%

commit v1 on v0

--- a/solution.py
+++ b/solution.py
@@ -108,7 +108,7 @@
         back_out[slot_index.reshape(-1)].reshape(tok_rows, per_token, width).astype(jnp.float32)
     )
     gate_part = jnp.sum(cotangent.astype(jnp.float32)[:, None, :] * out_rows, axis=2)
-    grad_gates = lax.psum(gate_part, "et")
+    grad_gates = jnp.sum(lax.all_gather(gate_part, "et"), axis=0)
     return (mixed, grad_tokens, grad_gates, grad_gate_w, grad_up_w, grad_down)
 
 

time: 296 us -> 284 us (0.959)
  blocking collectives: 86 us -> 73.6 us
    psum x1 -> x0, blocking collectives: 25.5 us -> none  [local(): grad_gates = lax.psum(gate_part, 'et')]
    all_gather x0 -> x1, blocking collectives: none -> 13.1 us  [local(): grad_gates = jnp.sum(lax.all_gather(gate_part, 'et'), axis=0)]
  transfers between devices with their start and end apart: 6 -> 6, of which waited for: 4 -> 4; matrix products, arithmetic and copies ran while one was open for 17% -> 18% of each run, Pallas kernels for 0% -> 0%
where the time goes in v1:
time: 284 us; the launch traced here: 282 us
  waiting for transfers between devices  105 us (37%)
  blocking collectives  73.6 us (26%)
  matrix products  46.7 us (16%)
  starting transfers between devices  20.7 us (7%)
  local copies, waits for them, and re-layouts  19.9 us (7%)
  between operations  14.1 us (5%)
    all_gather x1, waiting for transfers between devices, local(): expert_cot = lax.all_gather(expert_cot_part, 'et', axis=0)  37.7 us
    reduce_scatter x1, waiting for transfers between devices, local(): in_sum = lax.psum_scatter(in_part, 'et', scatter_dimension=2, tiled=True)  34.5 us
    all_to_all x1, blocking collectives, local(): lax.all_to_all(picked.reshape(experts, capacity, width), 'dp', split_axis...  33.9 us
    all_to_all x1, blocking collectives, local(): lax.all_to_all(scaled.reshape(experts, capacity, width), 'dp', split_axis...  26.7 us
    reduce_scatter x1, waiting for transfers between devices, local(): lax.psum_scatter(out_part.astype(jnp.bfloat16), 'et', scatter_dimension=2...  22.3 us
    all_gather x1, blocking collectives, local(): grad_gates = jnp.sum(lax.all_gather(gate_part, 'et'), axis=0)  13.1 us
    all_gather x1, waiting for transfers between devices, local(): expert_in = lax.all_gather(expert_in_part, 'et', axis=0)  10.9 us
    all_to_all x1, starting transfers between devices, local(): lax.all_to_all(out_sum, 'dp', split_axis=1, concat_axis=0, tiled=True)  10.2 us
  transfers between devices with their start and end apart: 6, of which 4 were waited for; matrix products, arithmetic and copies ran while one was open for 18% of the time, Pallas kernels for 0%

profile of v1, /device:TPU:2, one launch (start us, length us, event | category | flops | bytes accessed | tf_op | source)
XLA Modules:
  0.0 282.0 jit_solution(17248986702839260855)
XLA Ops:
  8.8 1.3 fusion.11
  10.5 33.9 %all_to_all.60 = bf16[64,24,256]{2,1,0:T(8,128)(2,1)S(1)} all-to-all(bf16[64,24,256]{2,1,0:T(8,128)(2,1)S(1)} %bitcast.95), channel_id=1, replica_groups=mesh['dp'=32,'et'=8] {'dp'}, dimensions={0} | all-to-all | bytes 1572864 | tf_op jit(solution)/shard_map/all_to_all | solution.py:50
  47.2 26.7 %all_to_all.61 = bf16[64,24,256]{2,1,0:T(8,128)(2,1)S(1)} all-to-all(bf16[64,24,256]{2,1,0:T(8,128)(2,1)S(1)} %bitcast.96), channel_id=1, replica_groups=mesh['dp'=32,'et'=8] {'dp'}, dimensions={0} | all-to-all | bytes 1572864 | tf_op jit(solution)/shard_map/all_to_all | solution.py:53
  74.9 10.9 %all-gather.4.cloned.1.call-done = bf16[8,2,768,256]{3,2,0,1:T(8,128)(2,1)} async-done(((bf16[1,2,768,256]{3,2,0,1:T(8,128)(2,1)}), bf16[8,2,768,256]{3,2,0,1:T(8,128)(2,1)}) %all-gather.4.cloned.1.call-update) | async-done | bytes 6291472 | tf_op jit(solution)/shard_map/all_gather | solution.py:57
  85.8 5.6 %convolution_bitcast_fusion.1 = f32[2,768,128]{2,1,0:T(8,128)} fusion(bf16[8,2,768,256]{3,2,0,1:T(8,128)(2,1)} %all-gather.4.cloned.1.call-done, bf16[2,8,256,128]{3,2,1,0:T(8,128)(2,1)S(1)} %bitcast.88), kind=kOutput, calls=%fused_computation.16 | convolution fusion | flops 805306368 | bytes 8126464 | tf_op jit(solution)/shard_map/jesd,ejdf->esf/dot_general | solution.py:63
  91.4 2.7 convolution_bitcast_fusion.2
  94.1 37.7 %all-gather.6.cloned.1.call-done = bf16[8,2,768,256]{3,2,0,1:T(8,128)(2,1)} async-done(((bf16[1,2,768,256]{3,2,0,1:T(8,128)(2,1)}), bf16[8,2,768,256]{3,2,0,1:T(8,128)(2,1)}) %all-gather.6.cloned.1.call-update) | async-done | bytes 6291472 | tf_op jit(solution)/shard_map/all_gather | solution.py:58
  131.7 5.7 %multiply_convert_fusion = (bf16[2,768,128]{2,1,0:T(8,128)(2,1)}, bf16[2,768,128]{2,1,0:T(8,128)(2,1)S(1)}, bf16[2,768,128]{2,1,0:T(8,128)(2,1)S(1)}) fusion(f32[2,768,128]{2,1,0:T(8,128)} %convolution_bitcast_fusion.2, f32[2,768,128]{2,1,0:T(8,128)S(1)} %copy-done.11, bf16[8,2,768,256]{3,2,0,1:T(8,128)(2,1)} %all-gather.6.cloned.1.call-done, ...), kind=kOutput, calls=%fused_computation.26 | convolution fusion | flops 808255488 | bytes 10092544 | tf_op jit(solution)/shard_map/jesd,efjd->esf/dot_general | solution.py:68
  138.2 4.4 %convolution_convert_fusion = bf16[2,768,2048]{2,1,0:T(8,128)(2,1)} fusion(bf16[2,768,128]{2,1,0:T(8,128)(2,1)S(1)} %get-tuple-element.52, bf16[2,128,2048]{2,1,0:T(8,128)(2,1)S(1)} %copy-done.10), kind=kOutput, calls=%fused_computation.4 | convolution fusion | flops 808452096 | bytes 7733248 | tf_op jit(solution)/shard_map/esf,efd->esd/dot_general | solution.py:67
  142.8 5.6 %fusion.21 = f32[2,128,8,256]{1,3,2,0:T(8,128)S(1)} fusion(bf16[8,2,768,256]{3,2,0,1:T(8,128)(2,1)} %all-gather.6.cloned.1.call-done, bf16[2,768,128]{2,1,0:T(8,128)(2,1)} %copy-done.9), kind=kOutput, calls=%fused_computation.33 | convolution fusion | flops 805306368 | bytes 8781824 | tf_op jit(solution)/shard_map/esf,jesd->efjd/dot_general | solution.py:75
  148.5 6.8 %fusion.23 = f32[2,8,256,128]{3,2,1,0:T(8,128)} fusion(bf16[8,2,768,256]{3,2,0,1:T(8,128)(2,1)} %all-gather.4.cloned.1.call-done, bf16[2,768,128]{2,1,0:T(8,128)(2,1)} %get-tuple-element.50), kind=kOutput, calls=%fused_computation.35 | convolution fusion | flops 805306368 | bytes 8781824 | tf_op jit(solution)/shard_map/jesd,esf->ejdf/dot_general | solution.py:81
  155.3 4.0 %fusion.25 = f32[2,8,256,128]{3,2,1,0:T(8,128)} fusion(bf16[8,2,768,256]{3,2,0,1:T(8,128)(2,1)S(1)} %bitcast.84, bf16[2,768,128]{2,1,0:T(8,128)(2,1)S(1)} %get-tuple-element.51), kind=kOutput, calls=%fused_computation.37 | convolution fusion | flops 805306368 | bytes 8781824 | tf_op jit(solution)/shard_map/jesd,esf->ejdf/dot_general | solution.py:78
  159.3 1.8 fusion.42
  161.1 4.5 %add_convert_fusion = bf16[2,768,2048]{2,1,0:T(8,128)(2,1)} fusion(f32[2,768,2048]{2,1,0:T(8,128)S(1)} %fusion.42, bf16[2,768,128]{2,1,0:T(8,128)(2,1)S(1)} %copy-done.8, bf16[2,2048,128]{2,1,0:T(8,128)(2,1)S(1)} %copy-done.3), kind=kOutput, calls=%fused_computation.1 | convolution fusion | flops 811597824 | bytes 20316160 | tf_op jit(solution)/shard_map/esf,edf->esd/dot_general | solution.py:87
  165.6 22.3 %reduce-scatter.3.cloned.1.call-done = bf16[2,768,256]{2,1,0:T(8,128)(2,1)} async-done(((bf16[2,768,2048]{2,1,0:T(8,128)(2,1)}), bf16[2,768,256]{2,1,0:T(8,128)(2,1)}) %reduce-scatter.3.cloned.1.call-update) | async-done | bytes 786448 | tf_op jit(solution)/shard_map/reduce_scatter | solution.py:90
  187.9 3.0 %copy.98 = bf16[2,768,256]{2,0,1:T(2,128)(2,1)} copy(bf16[2,768,256]{2,1,0:T(8,128)(2,1)} %reduce-scatter.3.cloned.1.call-done) | data formatting | bytes 1572864 | tf_op jit(solution)/shard_map/reduce_scatter | solution.py:90
  190.9 10.2 %all-to-all-start.1 = ((bf16[2,768,256]{2,0,1:T(2,128)(2,1)}), bf16[2,768,256]{2,0,1:T(2,128)(2,1)}, u32[]{:S(2)}, u32[]{:S(2)}) async-start(bf16[2,768,256]{2,0,1:T(2,128)(2,1)} %copy.98), calls=%async_computation.2 | async-start | bytes 1572864 | tf_op jit(solution)/shard_map/all_to_all | solution.py:96
  201.1 34.5 %reduce-scatter.5.cloned.1.call-done = bf16[2,768,256]{2,1,0:T(8,128)(2,1)} async-done(((bf16[2,768,2048]{2,1,0:T(8,128)(2,1)}), bf16[2,768,256]{2,1,0:T(8,128)(2,1)}) %reduce-scatter.5.cloned.1.call-update) | async-done | bytes 786448 | tf_op jit(solution)/shard_map/reduce_scatter | solution.py:94
  235.6 2.8 copy.106
  238.4 10.2 %all-to-all-start.3 = ((bf16[2,768,256]{2,0,1:T(2,128)(2,1)}), bf16[2,768,256]{2,0,1:T(2,128)(2,1)}, u32[]{:S(2)}, u32[]{:S(2)}) async-start(bf16[2,768,256]{2,0,1:T(2,128)(2,1)} %copy.106), calls=%async_computation.5 | async-start | bytes 1572864 | tf_op jit(solution)/shard_map/all_to_all | solution.py:97
  251.0 1.8 copy.111
  252.8 1.3 copy.99
  254.1 3.9 %gather_fusion = bf16[1024,256]{1,0:T(8,128)(2,1)S(1)} fusion(bf16[1536,256]{1,0:T(8,128)(2,1)S(1)} %bitcast.85, s32[1024]{0:T(1024)S(1)} %broadcast_clamp_fusion), kind=kCustom, calls=%fused_computation | custom fusion | bytes 1052672 | tf_op jit(solution)/shard_map/gather | solution.py:108
  258.3 13.1 %all-gather = f32[1024,8]{1,0:T(8,128)S(1)} all-gather(f32[128,8]{1,0:T(8,128)S(1)} %fusion.18), channel_id=2, replica_groups=mesh['dp'=32,'et'=8] {'et'}, dimensions={0}, use_global_device_ids=true | all-gather | bytes 36864 | tf_op jit(solution)/shard_map/all_gather | solution.py:111
  (78 shorter events, 13.4 us)
Async XLA Ops:
  7.2 84.2 %copy-start = (bf16[2,2048,128]{2,1,0:T(8,128)(2,1)S(1)}, bf16[2,2048,128]{2,1,0:T(8,128)(2,1)}, u32[]{:S(2)}) copy-start(bf16[2,2048,128]{2,1,0:T(8,128)(2,1)} %param.11) | copy-start | bytes 3145732
  7.2 2.9 %copy-start.15 = (bf16[128,256]{1,0:T(8,128)(2,1)S(1)}, bf16[128,256]{1,0:T(8,128)(2,1)}, u32[]{:S(2)}) copy-start(bf16[128,256]{1,0:T(8,128)(2,1)} %param.7) | copy-start | bytes 196612
  7.2 78.6 %all-gather.4.cloned.1.call-start = ((), (), s32[]{:S(2)}) async-start(), calls=%async_computation.6 | async-start | bytes 7077888 | tf_op jit(solution)/shard_map/all_gather | solution.py:57
  8.2 37.2 %copy-start.17 = (bf16[128,8]{0,1:T(8,128)(2,1)S(1)}, bf16[128,8]{0,1:T(8,128)(2,1)}, u32[]{:S(2)}) copy-start(bf16[128,8]{0,1:T(8,128)(2,1)} %param.10) | copy-start | bytes 6148
  10.1 35.2 %copy-start.4 = (bf16[1536,128]{1,0:T(8,128)(2,1)}, bf16[1536,128]{1,0:T(8,128)(2,1)S(1)}, u32[]{:S(2)}) copy-start(bf16[1536,128]{1,0:T(8,128)(2,1)S(1)} %fusion.11) | copy-start | bytes 1179652
  10.1 36.7 %copy-start.13 = (bf16[128,256]{1,0:T(8,128)(2,1)S(1)}, bf16[128,256]{1,0:T(8,128)(2,1)}, u32[]{:S(2)}) copy-start(bf16[128,256]{1,0:T(8,128)(2,1)} %param.8) | copy-start | bytes 196612
  45.3 40.5 %copy-start.2 = (bf16[2,2048,128]{2,1,0:T(8,128)(2,1)S(1)}, bf16[2,2048,128]{2,1,0:T(8,128)(2,1)}, u32[]{:S(2)}) copy-start(bf16[2,2048,128]{2,1,0:T(8,128)(2,1)} %param.12) | copy-start | bytes 3145732
  45.3 86.4 %all-gather.6.cloned.1.call-start = ((), (), s32[]{:S(2)}) async-start(), calls=%async_computation.8 | async-start | bytes 7077888 | tf_op jit(solution)/shard_map/all_gather | solution.py:58
  46.9 28.0 %copy-start.6 = (bf16[1536,128]{1,0:T(8,128)(2,1)}, bf16[1536,128]{1,0:T(8,128)(2,1)S(1)}, u32[]{:S(2)}) copy-start(bf16[1536,128]{1,0:T(8,128)(2,1)S(1)} %fusion.8) | copy-start | bytes 1179652
  74.9 113.0 %reduce-scatter.3.cloned.1.call-start = ((), (), s32[]{:S(2)}) async-start(), calls=%async_computation.7 | async-start | bytes 7077888 | tf_op jit(solution)/shard_map/reduce_scatter | solution.py:90
  85.8 5.6 %copy-start.1 = (bf16[8,2,768,256]{3,2,0,1:T(8,128)(2,1)S(1)}, bf16[8,2,768,256]{3,2,0,1:T(8,128)(2,1)}, u32[]{:S(2)}) copy-start(bf16[8,2,768,256]{3,2,0,1:T(8,128)(2,1)} %all-gather.4.cloned.1.call-done) | copy-start | bytes 18874372
  85.8 45.9 %copy-start.10 = (bf16[2,128,2048]{2,1,0:T(8,128)(2,1)S(1)}, bf16[2,128,2048]{2,1,0:T(8,128)(2,1)}, u32[]{:S(2)}) copy-start(bf16[2,128,2048]{2,1,0:T(8,128)(2,1)} %param.13) | copy-start | bytes 3145732
  91.4 40.3 %copy-start.11 = (f32[2,768,128]{2,1,0:T(8,128)S(1)}, f32[2,768,128]{2,1,0:T(8,128)}, u32[]{:S(2)}) copy-start(f32[2,768,128]{2,1,0:T(8,128)} %convolution_bitcast_fusion.1) | copy-start | bytes 2359300
  142.6 93.0 %reduce-scatter.5.cloned.1.call-start = ((), (), s32[]{:S(2)}) async-start(), calls=%async_computation.9 | async-start | bytes 7077888 | tf_op jit(solution)/shard_map/reduce_scatter | solution.py:94
  142.8 12.5 %slice-start = ((s8[6291456]{0:T(1024)(128)(4,1)}), s8[4194304]{0:T(1024)(128)(4,1)S(1)}, s32[]{:S(2)}) async-start(s8[6291456]{0:T(1024)(128)(4,1)} %bitcast.83), calls=%async_computation.10 | async-start | bytes 8388608
  148.5 6.8 %slice-start.1 = ((s8[6291456]{0:T(1024)(128)(4,1)}), s8[2097152]{0:T(1024)(128)(4,1)S(1)}, s32[]{:S(2)}) async-start(s8[6291456]{0:T(1024)(128)(4,1)} %bitcast.83), calls=%async_computation.11 | async-start | bytes 4194304
  159.3 1.8 copy-start.8
  165.6 83.1 %copy-start.14 = (bf16[128,256]{1,0:T(8,128)(2,1)S(1)}, bf16[128,256]{1,0:T(8,128)(2,1)}, u32[]{:S(2)}) copy-start(bf16[128,256]{1,0:T(8,128)(2,1)} %param.8) | copy-start | bytes 196612
  165.6 83.7 %copy-start.16 = (s32[128,8]{0,1:T(8,128)S(1)}, s32[128,8]{0,1:T(8,128)}, u32[]{:S(2)}) copy-start(s32[128,8]{0,1:T(8,128)} %param.9) | copy-start | bytes 12292
  190.9 47.5 %all-to-all-start.1 = ((bf16[2,768,256]{2,0,1:T(2,128)(2,1)}), bf16[2,768,256]{2,0,1:T(2,128)(2,1)}, u32[]{:S(2)}, u32[]{:S(2)}) async-start(bf16[2,768,256]{2,0,1:T(2,128)(2,1)} %copy.98), calls=%async_computation.2 | async-start | bytes 1572864 | tf_op jit(solution)/shard_map/all_to_all | solution.py:96
  238.4 34.7 %all-to-all-start.3 = ((bf16[2,768,256]{2,0,1:T(2,128)(2,1)}), bf16[2,768,256]{2,0,1:T(2,128)(2,1)}, u32[]{:S(2)}, u32[]{:S(2)}) async-start(bf16[2,768,256]{2,0,1:T(2,128)(2,1)} %copy.106), calls=%async_computation.5 | async-start | bytes 1572864 | tf_op jit(solution)/shard_map/all_to_all | solution.py:97
  249.3 22.9 %copy-start.7 = (bf16[1536,128]{1,0:T(8,128)(2,1)S(1)}, bf16[1536,128]{1,0:T(8,128)(2,1)}, u32[]{:S(2)}) copy-start(bf16[1536,128]{1,0:T(8,128)(2,1)} %copy-done.6) | copy-start | bytes 1179652
  252.8 5.3 %copy-start.12 = (f32[128,256]{1,0:T(8,128)S(1)}, f32[128,256]{1,0:T(8,128)}, u32[]{:S(2)}) copy-start(f32[128,256]{1,0:T(8,128)} %convert_element_type.85) | copy-start | bytes 393220
  252.8 21.6 %copy-start.5 = (bf16[1536,128]{1,0:T(8,128)(2,1)S(1)}, bf16[1536,128]{1,0:T(8,128)(2,1)}, u32[]{:S(2)}) copy-start(bf16[1536,128]{1,0:T(8,128)(2,1)} %copy-done.4) | copy-start | bytes 1179652
  (2 other events, 2.6 us)
Sparse Core Ops, SparseCore 0:
  45.4 40.3 all-gather.3
  88.2 43.4 all-gather.5
  142.7 45.1 reduce-scatter.2
  190.3 45.2 reduce-scatter.4
